TPU v7x, 32 devices: a whole 2x2x4 slice. The times are simulated.
32 devices in a mesh: parts: 2 (over x), rows: 2 (over core), cols: 8 (over z, y).
Axes of the slice: x: 2, y: 2, z: 4, core: 2. Of those that a mesh axis runs over, the one named last changes fastest.
Arguments:
- src_feat: float32 [32, 131072], P(None, ('parts', 'rows', 'cols')), parts along dimension 1, may hold values from -0.75 to 0.75
- tgt_feat: float32 [32, 16384], P(None, ('parts', 'cols')), parts along dimension 1, may hold values from -0.75 to 0.75
- tgt_pot: float32 [16384], P(('parts', 'cols')), parts along dimension 0, may hold values from -25 to 25
- log_src: float32 [131072], P(('parts', 'rows', 'cols')), parts along dimension 0, may hold values from -3 to 3
- log_tgt: float32 [16384], P(('parts', 'cols')), parts along dimension 0, may hold values from -3 to 3
- pairs: int32 [512, 24], P(('parts', 'rows', 'cols')), parts along dimension 0, may hold values from 0 to 31, as said below
- counts: int32 [512], P(('parts', 'rows', 'cols')), parts along dimension 0, may hold values from 1 to 24, as said below
Outputs:
- src_pot: float32 [131072], P(('parts', 'rows', 'cols')), parts along dimension 0
- new_tgt_pot: float32 [16384], P(('parts', 'cols')), parts along dimension 0
There are 2 independent parts, one for each index of `parts`. A program takes and returns all parts, laid end to end along the dimension named above; each array names one. Nothing has to cross between parts.
Inputs may be any that keep to these rules, and one draw needn't show every extreme that they name: `pairs`: each row names 24 different target blocks, and every target block is the first entry of some row. `counts`: row 0 uses all 24 entries and row 1 only one.
All inputs are finite; a program needn't handle non-finite values.
Results may differ from a plain program's by a relative error of at most 0.0003.
Values sent between devices are 32-bit elements; how exact they have to be, the bound alone decides.
No kernel may reach another device: no remote copies, remote signals or barrier semaphores. Data moves between devices by JAX's collectives and lax.ppermute only.
A program may use at most 128 MiB of HBM per device.

v0:
```python
import jax
import jax.numpy as jnp
from jax import lax
from jax.sharding import PartitionSpec as P

D = 32
BLK = 256
GROUP = 8
epsilon = 0.1
NEG = -1e30


def joined(array, axis, combine):
    everything = jax.tree.map(lambda part: lax.all_gather(part, axis), array)
    initial = jax.tree.map(lambda part: part[0], everything)

    def step(k, so_far):
        return combine(so_far, jax.tree.map(lambda part: part[k], everything))

    return lax.fori_loop(1, lax.axis_size(axis), step, initial)


def combine_parts(first, second):
    top = jnp.maximum(first[0], second[0])
    total = first[1] * jnp.exp(first[0] - top) + second[1] * jnp.exp(second[0] - top)
    return (top, total)


def on_device(src_feat, tgt_feat, tgt_pot, log_src, log_tgt, pairs, counts):
    own_targets = tgt_feat.shape[1]
    packed = jnp.concatenate([tgt_feat, tgt_pot[None, :], log_tgt[None, :]], axis=0)
    whole = lax.all_gather(packed, "cols", axis=1, tiled=True)
    feats = whole[:D]
    ynorm = jnp.sum(feats * feats, axis=0)
    tblocks = whole.shape[1] // BLK
    table = jnp.concatenate([whole, ynorm[None, :]], axis=0)
    blocks = jnp.transpose(table.reshape(D + 3, tblocks, BLK), (1, 0, 2))
    within = jnp.arange(GROUP, dtype=jnp.int32)
    block_numbers = jnp.arange(tblocks, dtype=jnp.int32)

    def row_step(carry, index):
        start = index * BLK
        xs = lax.dynamic_slice_in_dim(src_feat, start, BLK, 1)
        weights = lax.dynamic_slice_in_dim(log_src, start, BLK, 0)
        xnorm = jnp.sum(xs * xs, axis=0)
        row_ids = pairs[index]
        count = counts[index]
        ngroups = (count + GROUP - 1) // GROUP
        slabs = jnp.take(blocks, row_ids, axis=0)

        def take_group(step):
            ids = lax.dynamic_slice_in_dim(row_ids, step * GROUP, GROUP, 0)
            group = lax.dynamic_slice_in_dim(slabs, step * GROUP, GROUP, 0)
            mask = jnp.repeat(step * GROUP + within < count, BLK)
            cross = jnp.einsum(
                "dr,gdc->rgc",
                xs,
                group[:, :D, :],
                precision=lax.Precision.HIGHEST,
                preferred_element_type=jnp.float32,
            ).reshape(BLK, GROUP * BLK)
            cost = xnorm[:, None] + group[:, D + 2, :].reshape(-1)[None, :] - 2.0 * cross
            return (ids, mask, group, cost)

        def row_pass(step, state):
            run_top, run_sum = state
            ids, mask, group, cost = take_group(step)
            pots = group[:, D, :].reshape(-1)
            logs = group[:, D + 1, :].reshape(-1)
            scores = jnp.where(mask[None, :], logs[None, :] + (pots[None, :] - cost) / epsilon, NEG)
            top = jnp.maximum(run_top, jnp.max(scores, axis=1))
            run_sum = run_sum * jnp.exp(run_top - top) + jnp.sum(
                jnp.exp(scores - top[:, None]), axis=1
            )
            return (top, run_sum)

        start_state = (jnp.full((BLK,), NEG, jnp.float32), jnp.zeros((BLK,), jnp.float32))
        run_top, run_sum = lax.fori_loop(0, ngroups, row_pass, start_state)
        fpot = -epsilon * (run_top + jnp.log(run_sum))

        def col_pass(step, state):
            acc_top, acc_sum = state
            ids, mask, group, cost = take_group(step)
            scores = jnp.where(
                mask[None, :], weights[:, None] + (fpot[:, None] - cost) / epsilon, NEG
            )
            col_top = jnp.max(scores, axis=0)
            col_sum = jnp.where(mask, jnp.sum(jnp.exp(scores - col_top[None, :]), axis=0), 0.0)
            col_top = col_top.reshape(GROUP, BLK)
            col_sum = col_sum.reshape(GROUP, BLK)
            selector = ids[:, None] == block_numbers[None, :]
            onehot = selector.astype(jnp.float32)
            landed = jnp.max(jnp.where(selector[:, :, None], col_top[:, None, :], NEG), axis=0)
            top = jnp.maximum(acc_top, landed)
            top_here = jnp.einsum(
                "gt,tb->gb",
                onehot,
                top,
                precision=lax.Precision.HIGHEST,
                preferred_element_type=jnp.float32,
            )
            added = jnp.einsum(
                "gt,gb->tb",
                onehot,
                col_sum * jnp.exp(col_top - top_here),
                precision=lax.Precision.HIGHEST,
                preferred_element_type=jnp.float32,
            )
            fresh = acc_sum * jnp.exp(acc_top - top) + added
            return (top, fresh)

        carry = lax.fori_loop(0, ngroups, col_pass, carry)
        return (carry, fpot)

    init = (jnp.full((tblocks, BLK), NEG, jnp.float32), jnp.zeros((tblocks, BLK), jnp.float32))
    (acc_top, acc_sum), fblocks = lax.scan(
        row_step, init, jnp.arange(pairs.shape[0], dtype=jnp.int32)
    )
    src_pot = fblocks.reshape(-1)
    flat_top = acc_top.reshape(-1)
    flat_sum = acc_sum.reshape(-1)
    owner_start = lax.axis_index("cols") * own_targets
    all_top, all_sum = joined((flat_top, flat_sum), ("rows", "cols"), combine_parts)
    own_top = lax.dynamic_slice_in_dim(all_top, owner_start, own_targets, 0)
    own_sum = lax.dynamic_slice_in_dim(all_sum, owner_start, own_targets, 0)
    new_tgt_pot = -epsilon * (own_top + jnp.log(own_sum))
    return (src_pot, new_tgt_pot)


def solution(mesh):
    placed = (
        P(None, ("parts", "rows", "cols")),
        P(None, ("parts", "cols")),
        P(("parts", "cols")),
        P(("parts", "rows", "cols")),
        P(("parts", "cols")),
        P(("parts", "rows", "cols"), None),
        P(("parts", "rows", "cols")),
    )
    return jax.shard_map(
        on_device,
        mesh=mesh,
        in_specs=placed,
        out_specs=(P(("parts", "rows", "cols")), P(("parts", "cols"))),
        check_vma=False,
    )
```

profile of v0, /device:TPU:0, one launch (start us, length us, event | category | flops | bytes accessed | tf_op | source)
XLA Modules:
  0.0 660.8 jit_solution(5542897578245292571)
XLA Ops:
  8.9 46.1 %all-gather.4.cloned.1.call-done = f32[34,8192]{1,0:T(8,128)} async-done(((f32[34,1024]{1,0:T(8,128)}), f32[34,8192]{1,0:T(8,128)}) %all-gather.4.cloned.1.call-update) | async-done | bytes 1114128 | tf_op jit(solution)/shard_map/all_gather | solution.py:32
  57.9 446.4 %while.113 = (s32[]{:T(128)}, f32[32,256]{1,0:T(8,128)S(1)}, f32[32,256]{1,0:T(8,128)S(1)}, f32[16,256]{1,0:T(8,128)S(1)}, s32[16]{0:T(128)S(1)}, /*index=5*/s32...) while((s32[]{:T(128)}, f32[32,256]{1,0:T(8,128)S(1)}, ...), condition=%wide.region_12.13_spmd.clone.clone, body=%wide.region_1.12_spmd.clone.clone.sunk | while | flops 415103776 | bytes 13110493 | solution.py:116
  65.5 12.1 %while.114 = (s32[]{:T(128)}, f32[256]{0:T(256)S(1)}, f32[256]{0:T(256)S(1)}, s32[]{:T(128)}, s32[8]{0:T(128)S(1)}, /*index=5*/s32[]{:T(128)}, f32[24,35,256]{2,...) while((s32[]{:T(128)}, f32[256]{0:T(256)S(1)}, ...), condition=%wide.region_6.6_spmd, body=%wide.region_3.5_spmd.sunk | while | flops 206570016 | bytes 4627243 | solution.py:78
  66.3 2.9 fusion.43
  70.3 2.9 fusion.43
  74.4 2.9 fusion.43
  78.4 12.5 %while.115 = (s32[]{:T(128)}, f32[32,256]{1,0:T(8,128)S(1)}, f32[32,256]{1,0:T(8,128)S(1)}, s32[]{:T(128)}, s32[24]{0:T(128)S(1)}, /*index=5*/s32[32]{0:T(128)S(...) while((s32[]{:T(128)}, f32[32,256]{1,0:T(8,128)S(1)}, ...), condition=%wide.region_11.11_spmd, body=%wide.region_7.10_spmd.sunk | while | flops 208300816 | bytes 4961095 | solution.py:112
  98.5 4.1 while.114
  103.4 4.1 while.115
  115.1 12.1 %while.114 = (s32[]{:T(128)}, f32[256]{0:T(256)S(1)}, f32[256]{0:T(256)S(1)}, s32[]{:T(128)}, s32[8]{0:T(128)S(1)}, /*index=5*/s32[]{:T(128)}, f32[24,35,256]{2,...) while((s32[]{:T(128)}, f32[256]{0:T(256)S(1)}, ...), condition=%wide.region_6.6_spmd, body=%wide.region_3.5_spmd.sunk | while | flops 206570016 | bytes 4627243 | solution.py:78
  119.9 2.9 fusion.43
  124.0 2.9 fusion.43
  128.0 12.5 %while.115 = (s32[]{:T(128)}, f32[32,256]{1,0:T(8,128)S(1)}, f32[32,256]{1,0:T(8,128)S(1)}, s32[]{:T(128)}, s32[24]{0:T(128)S(1)}, /*index=5*/s32[32]{0:T(128)S(...) while((s32[]{:T(128)}, f32[32,256]{1,0:T(8,128)S(1)}, ...), condition=%wide.region_11.11_spmd, body=%wide.region_7.10_spmd.sunk | while | flops 208300816 | bytes 4961095 | solution.py:112
  148.1 8.1 %while.114 = (s32[]{:T(128)}, f32[256]{0:T(256)S(1)}, f32[256]{0:T(256)S(1)}, s32[]{:T(128)}, s32[8]{0:T(128)S(1)}, /*index=5*/s32[]{:T(128)}, f32[24,35,256]{2,...) while((s32[]{:T(128)}, f32[256]{0:T(256)S(1)}, ...), condition=%wide.region_6.6_spmd, body=%wide.region_3.5_spmd.sunk | while | flops 206570016 | bytes 4627243 | solution.py:78
  157.0 8.3 %while.115 = (s32[]{:T(128)}, f32[32,256]{1,0:T(8,128)S(1)}, f32[32,256]{1,0:T(8,128)S(1)}, s32[]{:T(128)}, s32[24]{0:T(128)S(1)}, /*index=5*/s32[32]{0:T(128)S(...) while((s32[]{:T(128)}, f32[32,256]{1,0:T(8,128)S(1)}, ...), condition=%wide.region_11.11_spmd, body=%wide.region_7.10_spmd.sunk | while | flops 208300816 | bytes 4961095 | solution.py:112
  173.0 12.1 %while.114 = (s32[]{:T(128)}, f32[256]{0:T(256)S(1)}, f32[256]{0:T(256)S(1)}, s32[]{:T(128)}, s32[8]{0:T(128)S(1)}, /*index=5*/s32[]{:T(128)}, f32[24,35,256]{2,...) while((s32[]{:T(128)}, f32[256]{0:T(256)S(1)}, ...), condition=%wide.region_6.6_spmd, body=%wide.region_3.5_spmd.sunk | while | flops 206570016 | bytes 4627243 | solution.py:78
  173.7 2.9 fusion.43
  177.8 2.9 fusion.43
  185.9 12.5 %while.115 = (s32[]{:T(128)}, f32[32,256]{1,0:T(8,128)S(1)}, f32[32,256]{1,0:T(8,128)S(1)}, s32[]{:T(128)}, s32[24]{0:T(128)S(1)}, /*index=5*/s32[32]{0:T(128)S(...) while((s32[]{:T(128)}, f32[32,256]{1,0:T(8,128)S(1)}, ...), condition=%wide.region_11.11_spmd, body=%wide.region_7.10_spmd.sunk | while | flops 208300816 | bytes 4961095 | solution.py:112
  206.0 12.1 %while.114 = (s32[]{:T(128)}, f32[256]{0:T(256)S(1)}, f32[256]{0:T(256)S(1)}, s32[]{:T(128)}, s32[8]{0:T(128)S(1)}, /*index=5*/s32[]{:T(128)}, f32[24,35,256]{2,...) while((s32[]{:T(128)}, f32[256]{0:T(256)S(1)}, ...), condition=%wide.region_6.6_spmd, body=%wide.region_3.5_spmd.sunk | while | flops 206570016 | bytes 4627243 | solution.py:78
  206.8 2.9 fusion.43
  214.9 2.9 fusion.43
  218.9 12.5 %while.115 = (s32[]{:T(128)}, f32[32,256]{1,0:T(8,128)S(1)}, f32[32,256]{1,0:T(8,128)S(1)}, s32[]{:T(128)}, s32[24]{0:T(128)S(1)}, /*index=5*/s32[32]{0:T(128)S(...) while((s32[]{:T(128)}, f32[32,256]{1,0:T(8,128)S(1)}, ...), condition=%wide.region_11.11_spmd, body=%wide.region_7.10_spmd.sunk | while | flops 208300816 | bytes 4961095 | solution.py:112
  239.0 8.1 %while.114 = (s32[]{:T(128)}, f32[256]{0:T(256)S(1)}, f32[256]{0:T(256)S(1)}, s32[]{:T(128)}, s32[8]{0:T(128)S(1)}, /*index=5*/s32[]{:T(128)}, f32[24,35,256]{2,...) while((s32[]{:T(128)}, f32[256]{0:T(256)S(1)}, ...), condition=%wide.region_6.6_spmd, body=%wide.region_3.5_spmd.sunk | while | flops 206570016 | bytes 4627243 | solution.py:78
  239.8 2.9 fusion.43
  247.9 8.3 %while.115 = (s32[]{:T(128)}, f32[32,256]{1,0:T(8,128)S(1)}, f32[32,256]{1,0:T(8,128)S(1)}, s32[]{:T(128)}, s32[24]{0:T(128)S(1)}, /*index=5*/s32[32]{0:T(128)S(...) while((s32[]{:T(128)}, f32[32,256]{1,0:T(8,128)S(1)}, ...), condition=%wide.region_11.11_spmd, body=%wide.region_7.10_spmd.sunk | while | flops 208300816 | bytes 4961095 | solution.py:112
  263.8 12.1 %while.114 = (s32[]{:T(128)}, f32[256]{0:T(256)S(1)}, f32[256]{0:T(256)S(1)}, s32[]{:T(128)}, s32[8]{0:T(128)S(1)}, /*index=5*/s32[]{:T(128)}, f32[24,35,256]{2,...) while((s32[]{:T(128)}, f32[256]{0:T(256)S(1)}, ...), condition=%wide.region_6.6_spmd, body=%wide.region_3.5_spmd.sunk | while | flops 206570016 | bytes 4627243 | solution.py:78
  264.6 2.9 fusion.43
  268.7 2.9 fusion.43
  272.7 2.9 fusion.43
  276.8 12.5 %while.115 = (s32[]{:T(128)}, f32[32,256]{1,0:T(8,128)S(1)}, f32[32,256]{1,0:T(8,128)S(1)}, s32[]{:T(128)}, s32[24]{0:T(128)S(1)}, /*index=5*/s32[32]{0:T(128)S(...) while((s32[]{:T(128)}, f32[32,256]{1,0:T(8,128)S(1)}, ...), condition=%wide.region_11.11_spmd, body=%wide.region_7.10_spmd.sunk | while | flops 208300816 | bytes 4961095 | solution.py:112
  296.9 8.1 %while.114 = (s32[]{:T(128)}, f32[256]{0:T(256)S(1)}, f32[256]{0:T(256)S(1)}, s32[]{:T(128)}, s32[8]{0:T(128)S(1)}, /*index=5*/s32[]{:T(128)}, f32[24,35,256]{2,...) while((s32[]{:T(128)}, f32[256]{0:T(256)S(1)}, ...), condition=%wide.region_6.6_spmd, body=%wide.region_3.5_spmd.sunk | while | flops 206570016 | bytes 4627243 | solution.py:78
  297.7 2.9 fusion.43
  305.8 8.3 %while.115 = (s32[]{:T(128)}, f32[32,256]{1,0:T(8,128)S(1)}, f32[32,256]{1,0:T(8,128)S(1)}, s32[]{:T(128)}, s32[24]{0:T(128)S(1)}, /*index=5*/s32[32]{0:T(128)S(...) while((s32[]{:T(128)}, f32[32,256]{1,0:T(8,128)S(1)}, ...), condition=%wide.region_11.11_spmd, body=%wide.region_7.10_spmd.sunk | while | flops 208300816 | bytes 4961095 | solution.py:112
  321.7 8.1 %while.114 = (s32[]{:T(128)}, f32[256]{0:T(256)S(1)}, f32[256]{0:T(256)S(1)}, s32[]{:T(128)}, s32[8]{0:T(128)S(1)}, /*index=5*/s32[]{:T(128)}, f32[24,35,256]{2,...) while((s32[]{:T(128)}, f32[256]{0:T(256)S(1)}, ...), condition=%wide.region_6.6_spmd, body=%wide.region_3.5_spmd.sunk | while | flops 206570016 | bytes 4627243 | solution.py:78
  322.5 2.9 fusion.43
  326.5 2.9 fusion.43
  330.6 8.3 %while.115 = (s32[]{:T(128)}, f32[32,256]{1,0:T(8,128)S(1)}, f32[32,256]{1,0:T(8,128)S(1)}, s32[]{:T(128)}, s32[24]{0:T(128)S(1)}, /*index=5*/s32[32]{0:T(128)S(...) while((s32[]{:T(128)}, f32[32,256]{1,0:T(8,128)S(1)}, ...), condition=%wide.region_11.11_spmd, body=%wide.region_7.10_spmd.sunk | while | flops 208300816 | bytes 4961095 | solution.py:112
  346.5 8.1 %while.114 = (s32[]{:T(128)}, f32[256]{0:T(256)S(1)}, f32[256]{0:T(256)S(1)}, s32[]{:T(128)}, s32[8]{0:T(128)S(1)}, /*index=5*/s32[]{:T(128)}, f32[24,35,256]{2,...) while((s32[]{:T(128)}, f32[256]{0:T(256)S(1)}, ...), condition=%wide.region_6.6_spmd, body=%wide.region_3.5_spmd.sunk | while | flops 206570016 | bytes 4627243 | solution.py:78
  347.3 2.9 fusion.43
  351.3 2.9 fusion.43
  355.4 8.3 %while.115 = (s32[]{:T(128)}, f32[32,256]{1,0:T(8,128)S(1)}, f32[32,256]{1,0:T(8,128)S(1)}, s32[]{:T(128)}, s32[24]{0:T(128)S(1)}, /*index=5*/s32[32]{0:T(128)S(...) while((s32[]{:T(128)}, f32[32,256]{1,0:T(8,128)S(1)}, ...), condition=%wide.region_11.11_spmd, body=%wide.region_7.10_spmd.sunk | while | flops 208300816 | bytes 4961095 | solution.py:112
  371.3 8.1 %while.114 = (s32[]{:T(128)}, f32[256]{0:T(256)S(1)}, f32[256]{0:T(256)S(1)}, s32[]{:T(128)}, s32[8]{0:T(128)S(1)}, /*index=5*/s32[]{:T(128)}, f32[24,35,256]{2,...) while((s32[]{:T(128)}, f32[256]{0:T(256)S(1)}, ...), condition=%wide.region_6.6_spmd, body=%wide.region_3.5_spmd.sunk | while | flops 206570016 | bytes 4627243 | solution.py:78
  372.1 2.9 fusion.43
  376.2 2.9 fusion.43
  380.2 8.3 %while.115 = (s32[]{:T(128)}, f32[32,256]{1,0:T(8,128)S(1)}, f32[32,256]{1,0:T(8,128)S(1)}, s32[]{:T(128)}, s32[24]{0:T(128)S(1)}, /*index=5*/s32[32]{0:T(128)S(...) while((s32[]{:T(128)}, f32[32,256]{1,0:T(8,128)S(1)}, ...), condition=%wide.region_11.11_spmd, body=%wide.region_7.10_spmd.sunk | while | flops 208300816 | bytes 4961095 | solution.py:112
  396.1 8.1 %while.114 = (s32[]{:T(128)}, f32[256]{0:T(256)S(1)}, f32[256]{0:T(256)S(1)}, s32[]{:T(128)}, s32[8]{0:T(128)S(1)}, /*index=5*/s32[]{:T(128)}, f32[24,35,256]{2,...) while((s32[]{:T(128)}, f32[256]{0:T(256)S(1)}, ...), condition=%wide.region_6.6_spmd, body=%wide.region_3.5_spmd.sunk | while | flops 206570016 | bytes 4627243 | solution.py:78
  396.9 2.9 fusion.43
  401.0 2.9 fusion.43
  405.0 8.3 %while.115 = (s32[]{:T(128)}, f32[32,256]{1,0:T(8,128)S(1)}, f32[32,256]{1,0:T(8,128)S(1)}, s32[]{:T(128)}, s32[24]{0:T(128)S(1)}, /*index=5*/s32[32]{0:T(128)S(...) while((s32[]{:T(128)}, f32[32,256]{1,0:T(8,128)S(1)}, ...), condition=%wide.region_11.11_spmd, body=%wide.region_7.10_spmd.sunk | while | flops 208300816 | bytes 4961095 | solution.py:112
  421.0 12.1 %while.114 = (s32[]{:T(128)}, f32[256]{0:T(256)S(1)}, f32[256]{0:T(256)S(1)}, s32[]{:T(128)}, s32[8]{0:T(128)S(1)}, /*index=5*/s32[]{:T(128)}, f32[24,35,256]{2,...) while((s32[]{:T(128)}, f32[256]{0:T(256)S(1)}, ...), condition=%wide.region_6.6_spmd, body=%wide.region_3.5_spmd.sunk | while | flops 206570016 | bytes 4627243 | solution.py:78
  421.8 2.9 fusion.43
  425.8 2.9 fusion.43
  429.8 2.9 fusion.43
  433.9 12.5 %while.115 = (s32[]{:T(128)}, f32[32,256]{1,0:T(8,128)S(1)}, f32[32,256]{1,0:T(8,128)S(1)}, s32[]{:T(128)}, s32[24]{0:T(128)S(1)}, /*index=5*/s32[32]{0:T(128)S(...) while((s32[]{:T(128)}, f32[32,256]{1,0:T(8,128)S(1)}, ...), condition=%wide.region_11.11_spmd, body=%wide.region_7.10_spmd.sunk | while | flops 208300816 | bytes 4961095 | solution.py:112
  454.0 12.1 %while.114 = (s32[]{:T(128)}, f32[256]{0:T(256)S(1)}, f32[256]{0:T(256)S(1)}, s32[]{:T(128)}, s32[8]{0:T(128)S(1)}, /*index=5*/s32[]{:T(128)}, f32[24,35,256]{2,...) while((s32[]{:T(128)}, f32[256]{0:T(256)S(1)}, ...), condition=%wide.region_6.6_spmd, body=%wide.region_3.5_spmd.sunk | while | flops 206570016 | bytes 4627243 | solution.py:78
  454.8 2.9 fusion.43
  462.9 2.9 fusion.43
  466.9 12.5 %while.115 = (s32[]{:T(128)}, f32[32,256]{1,0:T(8,128)S(1)}, f32[32,256]{1,0:T(8,128)S(1)}, s32[]{:T(128)}, s32[24]{0:T(128)S(1)}, /*index=5*/s32[32]{0:T(128)S(...) while((s32[]{:T(128)}, f32[32,256]{1,0:T(8,128)S(1)}, ...), condition=%wide.region_11.11_spmd, body=%wide.region_7.10_spmd.sunk | while | flops 208300816 | bytes 4961095 | solution.py:112
  487.0 8.1 %while.114 = (s32[]{:T(128)}, f32[256]{0:T(256)S(1)}, f32[256]{0:T(256)S(1)}, s32[]{:T(128)}, s32[8]{0:T(128)S(1)}, /*index=5*/s32[]{:T(128)}, f32[24,35,256]{2,...) while((s32[]{:T(128)}, f32[256]{0:T(256)S(1)}, ...), condition=%wide.region_6.6_spmd, body=%wide.region_3.5_spmd.sunk | while | flops 206570016 | bytes 4627243 | solution.py:78
  487.8 2.9 fusion.43
  495.9 8.3 %while.115 = (s32[]{:T(128)}, f32[32,256]{1,0:T(8,128)S(1)}, f32[32,256]{1,0:T(8,128)S(1)}, s32[]{:T(128)}, s32[24]{0:T(128)S(1)}, /*index=5*/s32[32]{0:T(128)S(...) while((s32[]{:T(128)}, f32[32,256]{1,0:T(8,128)S(1)}, ...), condition=%wide.region_11.11_spmd, body=%wide.region_7.10_spmd.sunk | while | flops 208300816 | bytes 4961095 | solution.py:112
  504.4 114.5 %all-gather.1 = f32[16,1,8192]{2,1,0:T(1,128)S(1)} all-gather(f32[1,1,8192]{2,1,0:T(1,128)S(1)} %reshape.237), channel_id=1, replica_groups=mesh['parts'=2,'rows'=2,'cols'=8] {'rows','cols'}, dimensions={0}, use_global_device_ids=true | all-gather | bytes 557056 | tf_op jit(solution)/shard_map/all_gather | solution.py:14
  619.2 31.4 %all-gather = f32[16,1,8192]{2,1,0:T(1,128)S(1)} all-gather(f32[1,1,8192]{2,1,0:T(1,128)S(1)} %reshape.235), channel_id=1, replica_groups=mesh['parts'=2,'rows'=2,'cols'=8] {'rows','cols'}, dimensions={0}, use_global_device_ids=true | all-gather | bytes 557056 | tf_op jit(solution)/shard_map/all_gather | solution.py:14
  (1066 shorter events, 316.6 us)
Async XLA Ops:
  7.2 47.8 %all-gather.4.cloned.1.call-start = ((), (), s32[]{:S(2)}) async-start(), calls=%async_computation | async-start | bytes 1474560 | tf_op jit(solution)/shard_map/all_gather | solution.py:32
  55.0 2.0 copy-start
  57.1 0.9 copy-start.1
Sparse Core Ops, SparseCore 0:
  10.2 44.7 all-gather.3
where the time goes:
time: 665 us; the launch traced here: 661 us
  matrix products  216 us (32%)
  blocking collectives  146 us (22%)
  other arithmetic  126 us (19%)
  loops' own time  59.5 us (9%)
  local copies, waits for them, and re-layouts  53.3 us (8%)
  waiting for transfers between devices  46.1 us (7%)
  between operations  14.2 us (2%)
    dot_general x76, matrix products, take_group(): jnp.einsum('dr,gdc->rgc', xs, group[:, :D, :], precision=lax.Precision.HI...  198 us
    all_gather x2, blocking collectives, joined(): everything = jax.tree.map(lambda part: lax.all_gather(part, axis), array)  146 us
    another operation x1, loops' own time, on_device(): lax.scan(row_step, init, jnp.arange(pairs.shape[0], dtype=jnp.int32))  53.5 us
    lt x76, other arithmetic, take_group(): mask = jnp.repeat(step * GROUP + within < count, BLK)  52.8 us
    all_gather x1, waiting for transfers between devices, on_device(): whole = lax.all_gather(packed, 'cols', axis=1, tiled=True)  46.1 us
    reduce_sum x38, other arithmetic, row_pass(): jnp.sum(jnp.exp(scores - top[:, None]), axis=1)  13.7 us
    select_n x32, other arithmetic, row_step(): slabs = jnp.take(blocks, row_ids, axis=0)  13.3 us
  transfers between devices with their start and end apart: 1, of which 1 were waited for; matrix products, arithmetic and copies ran while one was open for 0% of the time, Pallas kernels for 0%

commit v1 on v0

--- a/solution.py
+++ b/solution.py
@@ -8,6 +8,25 @@
 GROUP = 8
 epsilon = 0.1
 NEG = -1e30
+
+
+def ring_gather(x, axis, dim):
+    size, mine, rows = (lax.axis_size(axis), lax.axis_index(axis), x.shape[dim])
+    upward = [(i, (i + 1) % size) for i in range(size)]
+    left = [(i, (i - 1) % size) for i in range(size)]
+    out = jnp.zeros((*x.shape[:dim], size * rows, *x.shape[dim + 1 :]), x.dtype)
+    out = lax.dynamic_update_slice_in_dim(out, x, mine * rows, axis=dim)
+    from_left = from_right = x
+    half = size // 2
+    for step in range(1, half + 1):
+        from_left = lax.ppermute(from_left, axis, upward)
+        out = lax.dynamic_update_slice_in_dim(out, from_left, (mine - step) % size * rows, axis=dim)
+        if step < size - half:
+            from_right = lax.ppermute(from_right, axis, left)
+            out = lax.dynamic_update_slice_in_dim(
+                out, from_right, (mine + step) % size * rows, axis=dim
+            )
+    return out
 
 
 def joined(array, axis, combine):
@@ -29,7 +48,7 @@
 def on_device(src_feat, tgt_feat, tgt_pot, log_src, log_tgt, pairs, counts):
     own_targets = tgt_feat.shape[1]
     packed = jnp.concatenate([tgt_feat, tgt_pot[None, :], log_tgt[None, :]], axis=0)
-    whole = lax.all_gather(packed, "cols", axis=1, tiled=True)
+    whole = ring_gather(packed, "cols", 1)
     feats = whole[:D]
     ynorm = jnp.sum(feats * feats, axis=0)
     tblocks = whole.shape[1] // BLK

time: 665 us -> 625 us (0.940)
  waiting for transfers between devices: 46.1 us -> 19.5 us
  starting transfers between devices: 0.04 us -> 19.5 us
  between operations: 14.2 us -> 0.84 us
  other arithmetic: 126 us -> 115 us
    all_gather x1 -> x0, waiting for transfers between devices: 46.1 us -> none  [on_device(): whole = lax.all_gather(packed, 'cols', axis=1, tiled=True)]
    ppermute x0 -> x7, waiting for transfers between devices: none -> 19.5 us  [the longest x4 19.5 us: ring_gather(): from_left = lax.ppermute(from_left, axis, upward)]
    ppermute x0 -> x7, starting transfers between devices: none -> 19.5 us  [the longest x3 10.7 us: ring_gather(): from_right = lax.ppermute(from_right, axis, left)]
    lt x76, other arithmetic: 52.8 us -> 42.9 us  [take_group(): mask = jnp.repeat(step * GROUP + within < count, BLK)]
  transfers between devices with their start and end apart: 1 -> 7, of which waited for: 1 -> 4; matrix products, arithmetic and copies ran while one was open for 0% -> 0% of each run, Pallas kernels for 0% -> 0%
where the time goes in v1:
time: 625 us; the launch traced here: 621 us
  matrix products  216 us (35%)
  blocking collectives  141 us (23%)
  other arithmetic  115 us (18%)
  loops' own time  57.2 us (9%)
  local copies, waits for them, and re-layouts  51.2 us (8%)
  starting transfers between devices  19.5 us (3%)
  waiting for transfers between devices  19.5 us (3%)
    dot_general x76, matrix products, take_group(): jnp.einsum('dr,gdc->rgc', xs, group[:, :D, :], precision=lax.Precision.HI...  198 us
    all_gather x2, blocking collectives, joined(): everything = jax.tree.map(lambda part: lax.all_gather(part, axis), array)  141 us
    another operation x1, loops' own time, on_device(): lax.scan(row_step, init, jnp.arange(pairs.shape[0], dtype=jnp.int32))  51.3 us
    lt x76, other arithmetic, take_group(): mask = jnp.repeat(step * GROUP + within < count, BLK)  42.9 us
    ppermute x4, waiting for transfers between devices, ring_gather(): from_left = lax.ppermute(from_left, axis, upward)  19.5 us
    reduce_sum x38, other arithmetic, row_pass(): jnp.sum(jnp.exp(scores - top[:, None]), axis=1)  13.7 us
    select_n x32, other arithmetic, row_step(): slabs = jnp.take(blocks, row_ids, axis=0)  13.3 us
    reduce_sum x16, other arithmetic, row_step(): xnorm = jnp.sum(xs * xs, axis=0)  12.5 us
  transfers between devices with their start and end apart: 7, of which 4 were waited for; matrix products, arithmetic and copies ran while one was open for 0% of the time, Pallas kernels for 0%

profile of v1, /device:TPU:0, one launch (start us, length us, event | category | flops | bytes accessed | tf_op | source)
XLA Modules:
  0.0 620.8 jit_solution(15962627419167027179)
XLA Ops:
  1.7 3.0 collective-permute-start
  4.7 3.1 collective-permute-start.1
  7.8 4.2 collective-permute-done
  14.2 3.6 collective-permute-start.3
  17.8 4.1 collective-permute-done.2
  24.4 3.9 collective-permute-start.5
  28.4 4.5 collective-permute-done.4
  34.2 6.7 %collective-permute-done.6 = f32[34,1024]{1,0:T(8,128)S(1)} collective-permute-done((f32[34,1024]{1,0:T(8,128)S(1)}, f32[34,1024]{1,0:T(8,128)S(1)}, u32[]{:S(2)}, u32[]{:S(2)}) %collective-permute-start.6) | collective-permute-done | bytes 139296 | tf_op jit(solution)/shard_map/ppermute | solution.py:22
  42.5 433.4 %while.113 = (s32[]{:T(128)}, f32[32,256]{1,0:T(8,128)S(1)}, f32[32,256]{1,0:T(8,128)S(1)}, f32[16,256]{1,0:T(8,128)S(1)}, s32[16]{0:T(128)S(1)}, /*index=5*/s32...) while((s32[]{:T(128)}, f32[32,256]{1,0:T(8,128)S(1)}, ...), condition=%wide.region_12.13_spmd.clone.clone, body=%wide.region_1.12_spmd.clone.clone.sunk | while | flops 415103776 | bytes 13110493 | solution.py:135
  49.8 11.8 %while.114 = (s32[]{:T(128)}, f32[256]{0:T(256)S(1)}, f32[256]{0:T(256)S(1)}, s32[]{:T(128)}, s32[8]{0:T(128)S(1)}, /*index=5*/s32[]{:T(128)}, f32[24,35,256]{2,...) while((s32[]{:T(128)}, f32[256]{0:T(256)S(1)}, ...), condition=%wide.region_6.6_spmd, body=%wide.region_3.5_spmd.sunk | while | flops 206570016 | bytes 4627243 | solution.py:97
  50.5 2.9 fusion.43
  54.4 2.9 fusion.43
  58.3 2.9 fusion.43
  62.4 12.1 %while.115 = (s32[]{:T(128)}, f32[32,256]{1,0:T(8,128)S(1)}, f32[32,256]{1,0:T(8,128)S(1)}, s32[]{:T(128)}, s32[24]{0:T(128)S(1)}, /*index=5*/s32[32]{0:T(128)S(...) while((s32[]{:T(128)}, f32[32,256]{1,0:T(8,128)S(1)}, ...), condition=%wide.region_11.11_spmd, body=%wide.region_7.10_spmd.sunk | while | flops 208300816 | bytes 4961095 | solution.py:131
  81.9 3.9 while.114
  82.5 2.9 fusion.43
  86.6 4.0 while.115
  98.0 11.8 %while.114 = (s32[]{:T(128)}, f32[256]{0:T(256)S(1)}, f32[256]{0:T(256)S(1)}, s32[]{:T(128)}, s32[8]{0:T(128)S(1)}, /*index=5*/s32[]{:T(128)}, f32[24,35,256]{2,...) while((s32[]{:T(128)}, f32[256]{0:T(256)S(1)}, ...), condition=%wide.region_6.6_spmd, body=%wide.region_3.5_spmd.sunk | while | flops 206570016 | bytes 4627243 | solution.py:97
  98.7 2.9 fusion.43
  102.6 2.9 fusion.43
  106.5 2.9 fusion.43
  110.6 12.1 %while.115 = (s32[]{:T(128)}, f32[32,256]{1,0:T(8,128)S(1)}, f32[32,256]{1,0:T(8,128)S(1)}, s32[]{:T(128)}, s32[24]{0:T(128)S(1)}, /*index=5*/s32[32]{0:T(128)S(...) while((s32[]{:T(128)}, f32[32,256]{1,0:T(8,128)S(1)}, ...), condition=%wide.region_11.11_spmd, body=%wide.region_7.10_spmd.sunk | while | flops 208300816 | bytes 4961095 | solution.py:131
  130.1 7.8 %while.114 = (s32[]{:T(128)}, f32[256]{0:T(256)S(1)}, f32[256]{0:T(256)S(1)}, s32[]{:T(128)}, s32[8]{0:T(128)S(1)}, /*index=5*/s32[]{:T(128)}, f32[24,35,256]{2,...) while((s32[]{:T(128)}, f32[256]{0:T(256)S(1)}, ...), condition=%wide.region_6.6_spmd, body=%wide.region_3.5_spmd.sunk | while | flops 206570016 | bytes 4627243 | solution.py:97
  130.7 2.9 fusion.43
  134.7 2.9 fusion.43
  138.7 8.1 %while.115 = (s32[]{:T(128)}, f32[32,256]{1,0:T(8,128)S(1)}, f32[32,256]{1,0:T(8,128)S(1)}, s32[]{:T(128)}, s32[24]{0:T(128)S(1)}, /*index=5*/s32[32]{0:T(128)S(...) while((s32[]{:T(128)}, f32[32,256]{1,0:T(8,128)S(1)}, ...), condition=%wide.region_11.11_spmd, body=%wide.region_7.10_spmd.sunk | while | flops 208300816 | bytes 4961095 | solution.py:131
  154.2 11.8 %while.114 = (s32[]{:T(128)}, f32[256]{0:T(256)S(1)}, f32[256]{0:T(256)S(1)}, s32[]{:T(128)}, s32[8]{0:T(128)S(1)}, /*index=5*/s32[]{:T(128)}, f32[24,35,256]{2,...) while((s32[]{:T(128)}, f32[256]{0:T(256)S(1)}, ...), condition=%wide.region_6.6_spmd, body=%wide.region_3.5_spmd.sunk | while | flops 206570016 | bytes 4627243 | solution.py:97
  154.8 2.9 fusion.43
  158.8 2.9 fusion.43
  162.7 2.9 fusion.43
  166.7 12.1 %while.115 = (s32[]{:T(128)}, f32[32,256]{1,0:T(8,128)S(1)}, f32[32,256]{1,0:T(8,128)S(1)}, s32[]{:T(128)}, s32[24]{0:T(128)S(1)}, /*index=5*/s32[32]{0:T(128)S(...) while((s32[]{:T(128)}, f32[32,256]{1,0:T(8,128)S(1)}, ...), condition=%wide.region_11.11_spmd, body=%wide.region_7.10_spmd.sunk | while | flops 208300816 | bytes 4961095 | solution.py:131
  186.3 11.8 %while.114 = (s32[]{:T(128)}, f32[256]{0:T(256)S(1)}, f32[256]{0:T(256)S(1)}, s32[]{:T(128)}, s32[8]{0:T(128)S(1)}, /*index=5*/s32[]{:T(128)}, f32[24,35,256]{2,...) while((s32[]{:T(128)}, f32[256]{0:T(256)S(1)}, ...), condition=%wide.region_6.6_spmd, body=%wide.region_3.5_spmd.sunk | while | flops 206570016 | bytes 4627243 | solution.py:97
  186.9 2.9 fusion.43
  190.8 2.9 fusion.43
  194.7 2.9 fusion.43
  198.8 12.1 %while.115 = (s32[]{:T(128)}, f32[32,256]{1,0:T(8,128)S(1)}, f32[32,256]{1,0:T(8,128)S(1)}, s32[]{:T(128)}, s32[24]{0:T(128)S(1)}, /*index=5*/s32[32]{0:T(128)S(...) while((s32[]{:T(128)}, f32[32,256]{1,0:T(8,128)S(1)}, ...), condition=%wide.region_11.11_spmd, body=%wide.region_7.10_spmd.sunk | while | flops 208300816 | bytes 4961095 | solution.py:131
  218.3 7.8 %while.114 = (s32[]{:T(128)}, f32[256]{0:T(256)S(1)}, f32[256]{0:T(256)S(1)}, s32[]{:T(128)}, s32[8]{0:T(128)S(1)}, /*index=5*/s32[]{:T(128)}, f32[24,35,256]{2,...) while((s32[]{:T(128)}, f32[256]{0:T(256)S(1)}, ...), condition=%wide.region_6.6_spmd, body=%wide.region_3.5_spmd.sunk | while | flops 206570016 | bytes 4627243 | solution.py:97
  219.0 2.9 fusion.43
  227.0 8.1 %while.115 = (s32[]{:T(128)}, f32[32,256]{1,0:T(8,128)S(1)}, f32[32,256]{1,0:T(8,128)S(1)}, s32[]{:T(128)}, s32[24]{0:T(128)S(1)}, /*index=5*/s32[32]{0:T(128)S(...) while((s32[]{:T(128)}, f32[32,256]{1,0:T(8,128)S(1)}, ...), condition=%wide.region_11.11_spmd, body=%wide.region_7.10_spmd.sunk | while | flops 208300816 | bytes 4961095 | solution.py:131
  242.4 11.8 %while.114 = (s32[]{:T(128)}, f32[256]{0:T(256)S(1)}, f32[256]{0:T(256)S(1)}, s32[]{:T(128)}, s32[8]{0:T(128)S(1)}, /*index=5*/s32[]{:T(128)}, f32[24,35,256]{2,...) while((s32[]{:T(128)}, f32[256]{0:T(256)S(1)}, ...), condition=%wide.region_6.6_spmd, body=%wide.region_3.5_spmd.sunk | while | flops 206570016 | bytes 4627243 | solution.py:97
  255.0 12.1 %while.115 = (s32[]{:T(128)}, f32[32,256]{1,0:T(8,128)S(1)}, f32[32,256]{1,0:T(8,128)S(1)}, s32[]{:T(128)}, s32[24]{0:T(128)S(1)}, /*index=5*/s32[32]{0:T(128)S(...) while((s32[]{:T(128)}, f32[32,256]{1,0:T(8,128)S(1)}, ...), condition=%wide.region_11.11_spmd, body=%wide.region_7.10_spmd.sunk | while | flops 208300816 | bytes 4961095 | solution.py:131
  274.5 7.8 %while.114 = (s32[]{:T(128)}, f32[256]{0:T(256)S(1)}, f32[256]{0:T(256)S(1)}, s32[]{:T(128)}, s32[8]{0:T(128)S(1)}, /*index=5*/s32[]{:T(128)}, f32[24,35,256]{2,...) while((s32[]{:T(128)}, f32[256]{0:T(256)S(1)}, ...), condition=%wide.region_6.6_spmd, body=%wide.region_3.5_spmd.sunk | while | flops 206570016 | bytes 4627243 | solution.py:97
  279.1 2.9 fusion.43
  283.1 8.1 %while.115 = (s32[]{:T(128)}, f32[32,256]{1,0:T(8,128)S(1)}, f32[32,256]{1,0:T(8,128)S(1)}, s32[]{:T(128)}, s32[24]{0:T(128)S(1)}, /*index=5*/s32[32]{0:T(128)S(...) while((s32[]{:T(128)}, f32[32,256]{1,0:T(8,128)S(1)}, ...), condition=%wide.region_11.11_spmd, body=%wide.region_7.10_spmd.sunk | while | flops 208300816 | bytes 4961095 | solution.py:131
  298.6 7.8 %while.114 = (s32[]{:T(128)}, f32[256]{0:T(256)S(1)}, f32[256]{0:T(256)S(1)}, s32[]{:T(128)}, s32[8]{0:T(128)S(1)}, /*index=5*/s32[]{:T(128)}, f32[24,35,256]{2,...) while((s32[]{:T(128)}, f32[256]{0:T(256)S(1)}, ...), condition=%wide.region_6.6_spmd, body=%wide.region_3.5_spmd.sunk | while | flops 206570016 | bytes 4627243 | solution.py:97
  307.2 8.1 %while.115 = (s32[]{:T(128)}, f32[32,256]{1,0:T(8,128)S(1)}, f32[32,256]{1,0:T(8,128)S(1)}, s32[]{:T(128)}, s32[24]{0:T(128)S(1)}, /*index=5*/s32[32]{0:T(128)S(...) while((s32[]{:T(128)}, f32[32,256]{1,0:T(8,128)S(1)}, ...), condition=%wide.region_11.11_spmd, body=%wide.region_7.10_spmd.sunk | while | flops 208300816 | bytes 4961095 | solution.py:131
  322.7 7.8 %while.114 = (s32[]{:T(128)}, f32[256]{0:T(256)S(1)}, f32[256]{0:T(256)S(1)}, s32[]{:T(128)}, s32[8]{0:T(128)S(1)}, /*index=5*/s32[]{:T(128)}, f32[24,35,256]{2,...) while((s32[]{:T(128)}, f32[256]{0:T(256)S(1)}, ...), condition=%wide.region_6.6_spmd, body=%wide.region_3.5_spmd.sunk | while | flops 206570016 | bytes 4627243 | solution.py:97
  323.4 2.9 fusion.43
  331.3 8.1 %while.115 = (s32[]{:T(128)}, f32[32,256]{1,0:T(8,128)S(1)}, f32[32,256]{1,0:T(8,128)S(1)}, s32[]{:T(128)}, s32[24]{0:T(128)S(1)}, /*index=5*/s32[32]{0:T(128)S(...) while((s32[]{:T(128)}, f32[32,256]{1,0:T(8,128)S(1)}, ...), condition=%wide.region_11.11_spmd, body=%wide.region_7.10_spmd.sunk | while | flops 208300816 | bytes 4961095 | solution.py:131
  346.8 7.8 %while.114 = (s32[]{:T(128)}, f32[256]{0:T(256)S(1)}, f32[256]{0:T(256)S(1)}, s32[]{:T(128)}, s32[8]{0:T(128)S(1)}, /*index=5*/s32[]{:T(128)}, f32[24,35,256]{2,...) while((s32[]{:T(128)}, f32[256]{0:T(256)S(1)}, ...), condition=%wide.region_6.6_spmd, body=%wide.region_3.5_spmd.sunk | while | flops 206570016 | bytes 4627243 | solution.py:97
  347.5 2.9 fusion.43
  355.4 8.1 %while.115 = (s32[]{:T(128)}, f32[32,256]{1,0:T(8,128)S(1)}, f32[32,256]{1,0:T(8,128)S(1)}, s32[]{:T(128)}, s32[24]{0:T(128)S(1)}, /*index=5*/s32[32]{0:T(128)S(...) while((s32[]{:T(128)}, f32[32,256]{1,0:T(8,128)S(1)}, ...), condition=%wide.region_11.11_spmd, body=%wide.region_7.10_spmd.sunk | while | flops 208300816 | bytes 4961095 | solution.py:131
  370.9 7.8 %while.114 = (s32[]{:T(128)}, f32[256]{0:T(256)S(1)}, f32[256]{0:T(256)S(1)}, s32[]{:T(128)}, s32[8]{0:T(128)S(1)}, /*index=5*/s32[]{:T(128)}, f32[24,35,256]{2,...) while((s32[]{:T(128)}, f32[256]{0:T(256)S(1)}, ...), condition=%wide.region_6.6_spmd, body=%wide.region_3.5_spmd.sunk | while | flops 206570016 | bytes 4627243 | solution.py:97
  379.5 8.1 %while.115 = (s32[]{:T(128)}, f32[32,256]{1,0:T(8,128)S(1)}, f32[32,256]{1,0:T(8,128)S(1)}, s32[]{:T(128)}, s32[24]{0:T(128)S(1)}, /*index=5*/s32[32]{0:T(128)S(...) while((s32[]{:T(128)}, f32[32,256]{1,0:T(8,128)S(1)}, ...), condition=%wide.region_11.11_spmd, body=%wide.region_7.10_spmd.sunk | while | flops 208300816 | bytes 4961095 | solution.py:131
  395.0 11.8 %while.114 = (s32[]{:T(128)}, f32[256]{0:T(256)S(1)}, f32[256]{0:T(256)S(1)}, s32[]{:T(128)}, s32[8]{0:T(128)S(1)}, /*index=5*/s32[]{:T(128)}, f32[24,35,256]{2,...) while((s32[]{:T(128)}, f32[256]{0:T(256)S(1)}, ...), condition=%wide.region_6.6_spmd, body=%wide.region_3.5_spmd.sunk | while | flops 206570016 | bytes 4627243 | solution.py:97
  407.5 12.1 %while.115 = (s32[]{:T(128)}, f32[32,256]{1,0:T(8,128)S(1)}, f32[32,256]{1,0:T(8,128)S(1)}, s32[]{:T(128)}, s32[24]{0:T(128)S(1)}, /*index=5*/s32[32]{0:T(128)S(...) while((s32[]{:T(128)}, f32[32,256]{1,0:T(8,128)S(1)}, ...), condition=%wide.region_11.11_spmd, body=%wide.region_7.10_spmd.sunk | while | flops 208300816 | bytes 4961095 | solution.py:131
  427.1 11.8 %while.114 = (s32[]{:T(128)}, f32[256]{0:T(256)S(1)}, f32[256]{0:T(256)S(1)}, s32[]{:T(128)}, s32[8]{0:T(128)S(1)}, /*index=5*/s32[]{:T(128)}, f32[24,35,256]{2,...) while((s32[]{:T(128)}, f32[256]{0:T(256)S(1)}, ...), condition=%wide.region_6.6_spmd, body=%wide.region_3.5_spmd.sunk | while | flops 206570016 | bytes 4627243 | solution.py:97
  427.7 2.9 fusion.43
  435.6 2.9 fusion.43
  439.6 12.1 %while.115 = (s32[]{:T(128)}, f32[32,256]{1,0:T(8,128)S(1)}, f32[32,256]{1,0:T(8,128)S(1)}, s32[]{:T(128)}, s32[24]{0:T(128)S(1)}, /*index=5*/s32[32]{0:T(128)S(...) while((s32[]{:T(128)}, f32[32,256]{1,0:T(8,128)S(1)}, ...), condition=%wide.region_11.11_spmd, body=%wide.region_7.10_spmd.sunk | while | flops 208300816 | bytes 4961095 | solution.py:131
  459.1 7.8 %while.114 = (s32[]{:T(128)}, f32[256]{0:T(256)S(1)}, f32[256]{0:T(256)S(1)}, s32[]{:T(128)}, s32[8]{0:T(128)S(1)}, /*index=5*/s32[]{:T(128)}, f32[24,35,256]{2,...) while((s32[]{:T(128)}, f32[256]{0:T(256)S(1)}, ...), condition=%wide.region_6.6_spmd, body=%wide.region_3.5_spmd.sunk | while | flops 206570016 | bytes 4627243 | solution.py:97
  467.8 8.1 %while.115 = (s32[]{:T(128)}, f32[32,256]{1,0:T(8,128)S(1)}, f32[32,256]{1,0:T(8,128)S(1)}, s32[]{:T(128)}, s32[24]{0:T(128)S(1)}, /*index=5*/s32[32]{0:T(128)S(...) while((s32[]{:T(128)}, f32[32,256]{1,0:T(8,128)S(1)}, ...), condition=%wide.region_11.11_spmd, body=%wide.region_7.10_spmd.sunk | while | flops 208300816 | bytes 4961095 | solution.py:131
  475.9 109.6 %all-gather.1 = f32[16,1,8192]{2,1,0:T(1,128)S(1)} all-gather(f32[1,1,8192]{2,1,0:T(1,128)S(1)} %reshape.237), channel_id=1, replica_groups=mesh['parts'=2,'rows'=2,'cols'=8] {'rows','cols'}, dimensions={0}, use_global_device_ids=true | all-gather | bytes 557056 | tf_op jit(solution)/shard_map/all_gather | solution.py:33
  585.9 31.6 %all-gather = f32[16,1,8192]{2,1,0:T(1,128)S(1)} all-gather(f32[1,1,8192]{2,1,0:T(1,128)S(1)} %reshape.235), channel_id=1, replica_groups=mesh['parts'=2,'rows'=2,'cols'=8] {'rows','cols'}, dimensions={0}, use_global_device_ids=true | all-gather | bytes 557056 | tf_op jit(solution)/shard_map/all_gather | solution.py:33
  (1083 shorter events, 329.9 us)
Async XLA Ops:
  1.7 10.4 %collective-permute-start = (f32[34,1024]{1,0:T(8,128)S(1)}, f32[34,1024]{1,0:T(8,128)S(1)}, u32[]{:S(2)}, u32[]{:S(2)}) collective-permute-start(f32[34,1024]{1,0:T(8,128)S(1)} %get-tuple-element.724), channel_id=1, source_target_pairs={{0,1},{1,2},{2,3},{3,4},{4,5},{5,6},{6,7},{7,0},{8,9},{9,10},{10,1... | collective-permute-start | bytes 417800 | tf_op jit(solution)/shard_map/ppermute | solution.py:22
  4.7 9.5 %collective-permute-start.1 = (f32[34,1024]{1,0:T(8,128)S(1)}, f32[34,1024]{1,0:T(8,128)S(1)}, u32[]{:S(2)}, u32[]{:S(2)}) collective-permute-start(f32[34,1024]{1,0:T(8,128)S(1)} %get-tuple-element.724), channel_id=1, source_target_pairs={{0,7},{1,0},{2,1},{3,2},{4,3},{5,4},{6,5},{7,6},{8,15},{9,8},{10,9... | collective-permute-start | bytes 417800 | tf_op jit(solution)/shard_map/ppermute | solution.py:25
  12.1 9.9 %collective-permute-start.2 = (f32[34,1024]{1,0:T(8,128)S(1)}, f32[34,1024]{1,0:T(8,128)S(1)}, u32[]{:S(2)}, u32[]{:S(2)}) collective-permute-start(f32[34,1024]{1,0:T(8,128)S(1)} %collective-permute-done), channel_id=1, source_target_pairs={{0,1},{1,2},{2,3},{3,4},{4,5},{5,6},{6,7},{7,0},{8,9},{9,10},{10,1... | collective-permute-start | bytes 417800 | tf_op jit(solution)/shard_map/ppermute | solution.py:22
  14.2 10.2 %collective-permute-start.3 = (f32[34,1024]{1,0:T(8,128)S(1)}, f32[34,1024]{1,0:T(8,128)S(1)}, u32[]{:S(2)}, u32[]{:S(2)}) collective-permute-start(f32[34,1024]{1,0:T(8,128)S(1)} %collective-permute-done.1), channel_id=1, source_target_pairs={{0,7},{1,0},{2,1},{3,2},{4,3},{5,4},{6,5},{7,6},{8,15},{9,8},{10,9... | collective-permute-start | bytes 417800 | tf_op jit(solution)/shard_map/ppermute | solution.py:25
  21.9 10.9 %collective-permute-start.4 = (f32[34,1024]{1,0:T(8,128)S(1)}, f32[34,1024]{1,0:T(8,128)S(1)}, u32[]{:S(2)}, u32[]{:S(2)}) collective-permute-start(f32[34,1024]{1,0:T(8,128)S(1)} %collective-permute-done.2), channel_id=1, source_target_pairs={{0,1},{1,2},{2,3},{3,4},{4,5},{5,6},{6,7},{7,0},{8,9},{9,10},{10,1... | collective-permute-start | bytes 417800 | tf_op jit(solution)/shard_map/ppermute | solution.py:22
  24.4 9.7 %collective-permute-start.5 = (f32[34,1024]{1,0:T(8,128)S(1)}, f32[34,1024]{1,0:T(8,128)S(1)}, u32[]{:S(2)}, u32[]{:S(2)}) collective-permute-start(f32[34,1024]{1,0:T(8,128)S(1)} %collective-permute-done.3), channel_id=1, source_target_pairs={{0,7},{1,0},{2,1},{3,2},{4,3},{5,4},{6,5},{7,6},{8,15},{9,8},{10,9... | collective-permute-start | bytes 417800 | tf_op jit(solution)/shard_map/ppermute | solution.py:25
  32.9 8.0 %collective-permute-start.6 = (f32[34,1024]{1,0:T(8,128)S(1)}, f32[34,1024]{1,0:T(8,128)S(1)}, u32[]{:S(2)}, u32[]{:S(2)}) collective-permute-start(f32[34,1024]{1,0:T(8,128)S(1)} %collective-permute-done.4), channel_id=1, source_target_pairs={{0,1},{1,2},{2,3},{3,4},{4,5},{5,6},{6,7},{7,0},{8,9},{9,10},{10,1... | collective-permute-start | bytes 417800 | tf_op jit(solution)/shard_map/ppermute | solution.py:22
  41.6 0.9 copy-start
